TPU v7x, 32 devices: a whole 2x2x4 slice. The times are simulated.
32 devices in a mesh: grid: 8 (over y, x, core), band: 4 (over z).
Axes of the slice: x: 2, y: 2, z: 4, core: 2. Of those that a mesh axis runs over, the one named last changes fastest.
Arguments:
- occupied: bfloat16 [1024, 32, 24, 128], P('band', 'grid'), may hold values from -6 to 6
- potential: float32 [32, 24, 128], P('grid'), may hold values from 0.2 to 4
- shifts: float32 [64], P('band'), may hold values from 0.5 to 4
- source_term: float32 [64, 32, 24, 128], P('band', 'grid'), may hold values from -125 to 125
Outputs:
- solution: float32 [64, 32, 24, 128], P('band', 'grid')
- residual: float32 [64, 32, 24, 128], P('band', 'grid')
All inputs are finite; a program needn't handle non-finite values.
Results may differ from a plain program's by a relative error of at most 0.022.
Values may be sent and summed in bfloat16 or wider, within the bound.
No kernel may reach another device: no remote copies, remote signals or barrier semaphores. Data moves between devices by JAX's collectives and lax.ppermute only.
A program may use at most 128 MiB of HBM per device.

v0:
```python
import math
import jax
import jax.numpy as jnp
from jax import lax
from jax.sharding import PartitionSpec as P

ITERS = 2
COEFFICIENTS = (-205.0 / 72.0, 8.0 / 5.0, -1.0 / 5.0, 8.0 / 315.0, -1.0 / 560.0)


def with_halo(shard, sides, width):
    for axis, dim in sides:
        peers, length = (lax.axis_size(axis), shard.shape[dim])
        up = [(i, (i + 1) % peers) for i in range(peers - 1)]
        down = [(j, i) for i, j in up]
        last = lax.slice_in_dim(shard, length - width, length, axis=dim)
        leading = lax.slice_in_dim(shard, 0, width, axis=dim)
        before = lax.ppermute(last, axis, up)
        after = lax.ppermute(leading, axis, down)
        shard = jnp.concatenate([before, shard, after], axis=dim)
    return shard


def second_sum(padded, extent_x, extent_y, extent_z):
    middle = padded[:, 4 : 4 + extent_x, 4 : 4 + extent_y, 4 : 4 + extent_z]
    summed = 3.0 * COEFFICIENTS[0] * middle
    for offset in range(1, 5):
        along_x = (
            padded[:, 4 + offset : 4 + offset + extent_x, 4 : 4 + extent_y, 4 : 4 + extent_z]
            + padded[:, 4 - offset : 4 - offset + extent_x, 4 : 4 + extent_y, 4 : 4 + extent_z]
        )
        along_y = (
            padded[:, 4 : 4 + extent_x, 4 + offset : 4 + offset + extent_y, 4 : 4 + extent_z]
            + padded[:, 4 : 4 + extent_x, 4 - offset : 4 - offset + extent_y, 4 : 4 + extent_z]
        )
        along_z = (
            padded[:, 4 : 4 + extent_x, 4 : 4 + extent_y, 4 + offset : 4 + offset + extent_z]
            + padded[:, 4 : 4 + extent_x, 4 : 4 + extent_y, 4 - offset : 4 - offset + extent_z]
        )
        summed = (
            summed
            + COEFFICIENTS[offset] * along_x
            + COEFFICIENTS[offset] * along_y
            + COEFFICIENTS[offset] * along_z
        )
    return summed


def inner_product(first_field, second_field):
    return jnp.sum(first_field * second_field, axis=(1, 2, 3))


def expand(vector):
    return vector[:, None, None, None]


def body(occupied, potential, shifts, source_term):
    local_bands, width_x, width_y, width_z = source_term.shape
    local_occupied = occupied.shape[0]
    band_count = lax.axis_size("band")
    local_cells = width_x * width_y * width_z
    weight_scale = 2.0 / math.sqrt(
        local_occupied * band_count * local_cells * lax.axis_size("grid")
    )
    occupied_rows = occupied.reshape(local_occupied, local_cells)
    potential_shift = potential[None] + shifts[:, None, None, None]
    solution = jnp.zeros_like(source_term)
    residual = source_term
    direction = source_term
    norm_now = lax.psum(inner_product(source_term, source_term), "grid")
    for iteration in range(ITERS):
        padded = with_halo(direction.astype(jnp.bfloat16), (("grid", 1),), 4).astype(
            direction.dtype
        )
        padded = jnp.pad(padded, ((0, 0), (0, 0), (4, 4), (4, 4)))
        kinetic = -0.5 * second_sum(padded, width_x, width_y, width_z)
        rounded = direction.astype(jnp.bfloat16).reshape(local_bands, local_cells)
        partial_margin = lax.dot_general(
            occupied_rows,
            lax.all_gather(rounded, "band", axis=0, tiled=True),
            (((1,), (1,)), ((), ())),
            preferred_element_type=jnp.float32,
        )
        margins = lax.psum(partial_margin, "grid")
        scaled = (margins * weight_scale).astype(jnp.bfloat16)
        projected = lax.psum_scatter(
            lax.dot_general(
                scaled, occupied_rows, (((0,), (0,)), ((), ())), preferred_element_type=jnp.float32
            ).astype(jnp.bfloat16),
            "band",
            scatter_dimension=0,
            tiled=True,
        ).astype(jnp.float32)
        applied = kinetic + potential_shift * direction + projected.reshape(direction.shape)
        curvature = lax.psum(inner_product(direction, applied), "grid")
        step_size = norm_now / curvature
        solution = solution + expand(step_size) * direction
        residual = residual - expand(step_size) * applied
        if iteration + 1 < ITERS:
            norm_next = lax.psum(inner_product(residual, residual), "grid")
            direction = residual + expand(norm_next / norm_now) * direction
            norm_now = norm_next
    return (solution, residual)


def solution(mesh):
    in_specs = (
        P("band", "grid", None, None),
        P("grid", None, None),
        P("band"),
        P("band", "grid", None, None),
    )
    out_specs = (P("band", "grid", None, None), P("band", "grid", None, None))
    return jax.shard_map(body, mesh=mesh, in_specs=in_specs, out_specs=out_specs, check_vma=False)
```

profile of v0, /device:TPU:0, one launch (start us, length us, event | category | flops | bytes accessed | tf_op | source)
XLA Modules:
  0.0 345.8 jit_solution(5779249794180429042)
XLA Ops:
  9.4 40.6 %all-gather.3.cloned.1.call-done = bf16[64,12288]{1,0:T(8,128)(2,1)} async-done(((bf16[16,12288]{1,0:T(8,128)(2,1)}), bf16[64,12288]{1,0:T(8,128)(2,1)}) %all-gather.3.cloned.1.call-update) | async-done | bytes 1572880 | tf_op jit(solution)/shard_map/all_gather | solution.py:80
  50.0 5.8 %fusion.4 = f32[256,64]{1,0:T(8,128)} fusion(bf16[64,12288]{1,0:T(8,128)(2,1)} %all-gather.3.cloned.1.call-done, bf16[32,8,96,128]{3,2,1,0:T(8,128)(2,1)} %bitcast.35), kind=kOutput, calls=%fused_computation.38 | convolution fusion | flops 402653184 | bytes 7929856 | tf_op jit(solution)/shard_map/dot_general | solution.py:78
  55.9 51.9 %all-reduce.6.cloned.1.call-done = f32[256,64]{1,0:T(8,128)} async-done(((f32[256,64]{1,0:T(8,128)}), f32[256,64]{1,0:T(8,128)}) %all-reduce.6.cloned.1.call-update) | async-done | bytes 65552 | tf_op jit(solution)/shard_map/psum | solution.py:84
  107.8 6.2 %convolution_convert_fusion.1 = bf16[64,12288]{1,0:T(8,128)(2,1)} fusion(bf16[32,8,96,128]{3,2,1,0:T(8,128)(2,1)} %bitcast.36, f32[256,64]{1,0:T(8,128)} %all-reduce.6.cloned.1.call-done), kind=kOutput, calls=%fused_computation.33 | convolution fusion | flops 403472384 | bytes 7929856 | tf_op jit(solution)/shard_map/dot_general | solution.py:87
  114.0 1.4 collective-permute-start.1
  115.5 3.1 collective-permute-start
  118.5 1.3 collective-permute-done
  120.0 28.8 %reduce-scatter.3.cloned.1.call-done = bf16[16,12288]{1,0:T(8,128)(2,1)} async-done(((bf16[64,12288]{1,0:T(8,128)(2,1)}), bf16[16,12288]{1,0:T(8,128)(2,1)}) %reduce-scatter.3.cloned.1.call-update) | async-done | bytes 393232 | tf_op jit(solution)/shard_map/reduce_scatter | solution.py:86
  150.0 3.8 %multiply_reduce_fusion.2 = (f32[16]{0:T(128)S(1)}, f32[16]{0:T(128)S(1)}, f32[16,4,24,128]{3,2,1,0:T(8,128)}) fusion(f32[16,4,24,128]{3,2,1,0:T(8,128)S(1)} %copy-done, f32[16,4,24,128]{3,2,1,0:T(8,128)S(1)} %bitcast.41, f32[16]{0:T(128)S(1)} %copy-done.2, f32[4,24,128]{2,1,0:T(8,128)} %param.5, f32[16,12,24,128]{3,2,1,0:T(8,128)S(1)} %maximum_convert_fusion), kind=kLoop, calls=%fused_computation.135 | loop fusion | flops 9043936 | bytes 11846272 | tf_op jit(solution)/shard_map/reduce_sum | solution.py:50
  153.8 13.4 %all-reduce.2 = (f32[16]{0:T(128)S(1)}, f32[16]{0:T(128)S(1)}) all-reduce(f32[16]{0:T(128)S(1)} %get-tuple-element.3, f32[16]{0:T(128)S(1)} %get-tuple-element.2), channel_id=1, replica_groups=mesh['grid'=8,'band'=4] {'grid'}, use_global_device_ids=true, to_apply=%region_1.0 | all-reduce | flops 32 | bytes 256 | tf_op jit(solution)/shard_map/psum | solution.py:70
  167.3 1.4 multiply_reduce_fusion.1
  168.7 11.8 %psum.45 = f32[16]{0:T(128)S(1)} all-reduce(f32[16]{0:T(128)S(1)} %multiply_reduce_fusion.1), channel_id=1, replica_groups=mesh['grid'=8,'band'=4] {'grid'}, use_global_device_ids=true, to_apply=%region_7.8 | all-reduce | flops 16 | bytes 128 | tf_op jit(solution)/shard_map/psum | solution.py:100
  180.5 2.3 fusion.86
  183.7 34.6 %all-gather.5.cloned.1.call-done = bf16[64,12288]{1,0:T(8,128)(2,1)} async-done(((bf16[16,12288]{1,0:T(8,128)(2,1)}), bf16[64,12288]{1,0:T(8,128)(2,1)}) %all-gather.5.cloned.1.call-update) | async-done | bytes 1572880 | tf_op jit(solution)/shard_map/all_gather | solution.py:80
  218.3 5.9 %fusion.10 = f32[256,64]{1,0:T(8,128)} fusion(bf16[64,12288]{1,0:T(8,128)(2,1)} %all-gather.5.cloned.1.call-done, bf16[32,8,96,128]{3,2,1,0:T(8,128)(2,1)} %bitcast.37), kind=kOutput, calls=%fused_computation.46 | convolution fusion | flops 402653184 | bytes 7929856 | tf_op jit(solution)/shard_map/dot_general | solution.py:78
  224.3 51.9 %all-reduce.8.cloned.1.call-done = f32[256,64]{1,0:T(8,128)} async-done(((f32[256,64]{1,0:T(8,128)}), f32[256,64]{1,0:T(8,128)}) %all-reduce.8.cloned.1.call-update) | async-done | bytes 65552 | tf_op jit(solution)/shard_map/psum | solution.py:84
  276.2 6.2 %convolution_convert_fusion = bf16[64,12288]{1,0:T(8,128)(2,1)} fusion(bf16[32,8,96,128]{3,2,1,0:T(8,128)(2,1)} %bitcast.38, f32[256,64]{1,0:T(8,128)} %all-reduce.8.cloned.1.call-done), kind=kOutput, calls=%fused_computation.32 | convolution fusion | flops 403472384 | bytes 7929856 | tf_op jit(solution)/shard_map/dot_general | solution.py:87
  282.4 1.3 collective-permute-start.3
  283.7 3.1 collective-permute-start.2
  286.7 1.3 collective-permute-done.2
  288.2 29.0 %reduce-scatter.5.cloned.1.call-done = bf16[16,12288]{1,0:T(8,128)(2,1)} async-done(((bf16[64,12288]{1,0:T(8,128)(2,1)}), bf16[16,12288]{1,0:T(8,128)(2,1)}) %reduce-scatter.5.cloned.1.call-update) | async-done | bytes 393232 | tf_op jit(solution)/shard_map/reduce_scatter | solution.py:86
  318.5 3.9 %multiply_reduce_fusion = (f32[16]{0:T(128)S(1)}, f32[16,4,24,128]{3,2,1,0:T(8,128)}) fusion(f32[16,4,24,128]{3,2,1,0:T(8,128)S(1)} %copy-done.1, f32[16,4,24,128]{3,2,1,0:T(8,128)S(1)} %bitcast.42, f32[16]{0:T(128)S(1)} %copy-done.2, f32[4,24,128]{2,1,0:T(8,128)} %param.5, f32[16,12,24,128]{3,2,1,0:T(8,128)S(1)} %maximum_convert_fusion.1), kind=kLoop, calls=%fused_computation.131 | loop fusion | flops 8650736 | bytes 11846208 | tf_op jit(solution)/shard_map/reduce_sum | solution.py:50
  322.3 13.4 %psum.47 = f32[16]{0:T(128)S(1)} all-reduce(f32[16]{0:T(128)S(1)} %get-tuple-element.6), channel_id=1, replica_groups=mesh['grid'=8,'band'=4] {'grid'}, use_global_device_ids=true, to_apply=%region_11.12 | all-reduce | flops 16 | bytes 128 | tf_op jit(solution)/shard_map/psum | solution.py:95
  335.8 3.2 multiply_subtract_fusion
  (32 shorter events, 6.2 us)
Async XLA Ops:
  7.2 42.8 %all-gather.3.cloned.1.call-start = ((), (), s32[]{:S(2)}) async-start(), calls=%async_computation.2 | async-start | bytes 1966080 | tf_op jit(solution)/shard_map/all_gather | solution.py:80
  9.3 98.4 %all-reduce.6.cloned.1.call-start = ((), (), s32[]{:S(2)}) async-start(), calls=%async_computation.3 | async-start | bytes 262144 | tf_op jit(solution)/shard_map/psum | solution.py:84
  55.8 92.9 %reduce-scatter.3.cloned.1.call-start = ((), (), s32[]{:S(2)}) async-start(), calls=%async_computation.4 | async-start | bytes 1966080 | tf_op jit(solution)/shard_map/reduce_scatter | solution.py:86
  113.9 36.0 %copy-start = (f32[16,4,24,128]{3,2,1,0:T(8,128)S(1)}, f32[16,4,24,128]{3,2,1,0:T(8,128)}, u32[]{:S(2)}) copy-start(f32[16,4,24,128]{3,2,1,0:T(8,128)} %param.7) | copy-start | bytes 2359300
  114.0 36.0 %copy-start.2 = (f32[16]{0:T(128)S(1)}, f32[16]{0:T(128)}, u32[]{:S(2)}) copy-start(f32[16]{0:T(128)} %param.6) | copy-start | bytes 196
  114.0 104.4 %all-gather.5.cloned.1.call-start = ((), (), s32[]{:S(2)}) async-start(), calls=%async_computation.5 | async-start | bytes 1966080 | tf_op jit(solution)/shard_map/all_gather | solution.py:80
  114.0 4.5 %collective-permute-start.1 = (bf16[16,4,24,128]{3,2,1,0:T(8,128)(2,1)S(1)}, bf16[16,4,24,128]{3,2,1,0:T(8,128)(2,1)S(1)}, u32[]{:S(2)}, u32[]{:S(2)}) collective-permute-start(bf16[16,4,24,128]{3,2,1,0:T(8,128)(2,1)S(1)} %convert_element_type.31), channel_id=1, source_target_pairs={{4,0},{8,4},{12,8},{16,12},{20,16},{24,20},{28,24},{5,1},{9,5},{13... | collective-permute-start | bytes 1179656 | tf_op jit(solution)/shard_map/ppermute | solution.py:19
  115.5 4.4 %collective-permute-start = (bf16[16,4,24,128]{3,2,1,0:T(8,128)(2,1)S(1)}, bf16[16,4,24,128]{3,2,1,0:T(8,128)(2,1)S(1)}, u32[]{:S(2)}, u32[]{:S(2)}) collective-permute-start(bf16[16,4,24,128]{3,2,1,0:T(8,128)(2,1)S(1)} %convert_element_type.31), channel_id=1, source_target_pairs={{0,4},{4,8},{8,12},{12,16},{16,20},{20,24},{24,28},{1,5},{5,9},{9,... | collective-permute-start | bytes 1179656 | tf_op jit(solution)/shard_map/ppermute | solution.py:18
  183.7 92.5 %all-reduce.8.cloned.1.call-start = ((), (), s32[]{:S(2)}) async-start(), calls=%async_computation.6 | async-start | bytes 262144 | tf_op jit(solution)/shard_map/psum | solution.py:84
  224.2 93.0 %reduce-scatter.5.cloned.1.call-start = ((), (), s32[]{:S(2)}) async-start(), calls=%async_computation.7 | async-start | bytes 1966080 | tf_op jit(solution)/shard_map/reduce_scatter | solution.py:86
  282.4 4.4 %collective-permute-start.3 = (bf16[16,4,24,128]{3,2,1,0:T(8,128)(2,1)S(1)}, bf16[16,4,24,128]{3,2,1,0:T(8,128)(2,1)S(1)}, u32[]{:S(2)}, u32[]{:S(2)}) collective-permute-start(bf16[16,4,24,128]{3,2,1,0:T(8,128)(2,1)S(1)} %get-tuple-element.8), channel_id=1, source_target_pairs={{4,0},{8,4},{12,8},{16,12},{20,16},{24,20},{28,24},{5,1},{9,5},{13... | collective-permute-start | bytes 1179656 | tf_op jit(solution)/shard_map/ppermute | solution.py:19
  283.7 4.4 %collective-permute-start.2 = (bf16[16,4,24,128]{3,2,1,0:T(8,128)(2,1)S(1)}, bf16[16,4,24,128]{3,2,1,0:T(8,128)(2,1)S(1)}, u32[]{:S(2)}, u32[]{:S(2)}) collective-permute-start(bf16[16,4,24,128]{3,2,1,0:T(8,128)(2,1)S(1)} %get-tuple-element.8), channel_id=1, source_target_pairs={{0,4},{4,8},{8,12},{12,16},{16,20},{20,24},{24,28},{1,5},{5,9},{9,... | collective-permute-start | bytes 1179656 | tf_op jit(solution)/shard_map/ppermute | solution.py:18
  317.2 1.3 copy-start.1
Sparse Core Ops, SparseCore 0:
  10.1 39.7 all-gather.2
  56.0 51.7 all-reduce.5
  114.1 34.6 reduce-scatter.2
  183.8 34.4 all-gather.4
  224.4 51.7 all-reduce.7
  282.5 34.6 reduce-scatter.4
where the time goes:
time: 346 us
  waiting for transfers between devices  239 us (69%)
  blocking collectives  38.6 us (11%)
  matrix products  24 us (7%)
  other arithmetic  18.3 us (5%)
  between operations  14.2 us (4%)
  starting transfers between devices  9.07 us (3%)
    psum x2, waiting for transfers between devices, body(): margins = lax.psum(partial_margin, 'grid')  104 us
    all_gather x2, waiting for transfers between devices, body(): lax.all_gather(rounded, 'band', axis=0, tiled=True)  75.2 us
    reduce_scatter x2, waiting for transfers between devices, body(): lax.psum_scatter(lax.dot_general(scaled, occupied_rows, (((0,), (0,)), ((...  57.8 us
    psum x1, blocking collectives, body(): curvature = lax.psum(inner_product(direction, applied), 'grid')  13.4 us
    psum x1, blocking collectives, body(): norm_now = lax.psum(inner_product(source_term, source_term), 'grid')  13.4 us
    dot_general x2, matrix products, body(): lax.dot_general(scaled, occupied_rows, (((0,), (0,)), ((), ())), preferre...  12.3 us
    psum x1, blocking collectives, body(): norm_next = lax.psum(inner_product(residual, residual), 'grid')  11.8 us
    dot_general x2, matrix products, body(): lax.dot_general(occupied_rows, lax.all_gather(rounded, 'band', axis=0, ti...  11.7 us
  transfers between devices with their start and end apart: 10, of which 8 were waited for; matrix products, arithmetic and copies ran while one was open for 0% of the time, Pallas kernels for 0%

commit v1 on v0

--- a/solution.py
+++ b/solution.py
@@ -6,6 +6,27 @@
 
 ITERS = 2
 COEFFICIENTS = (-205.0 / 72.0, 8.0 / 5.0, -1.0 / 5.0, 8.0 / 315.0, -1.0 / 560.0)
+
+
+def joined_along(tiles, dim):
+    tiles = jnp.moveaxis(tiles, 0, dim)
+    shape = tiles.shape
+    return tiles.reshape(*shape[:dim], shape[dim] * shape[dim + 1], *shape[dim + 2 :])
+
+
+def grow_blocks(array, axis):
+    length, here = (lax.axis_size(axis), lax.axis_index(axis))
+    blocks, bit = (array[None], 1)
+    while bit < length:
+        other = lax.ppermute(blocks, axis, [(i, i ^ bit) for i in range(length)])
+        low = here & bit == 0
+        blocks = jnp.concatenate([jnp.where(low, blocks, other), jnp.where(low, other, blocks)])
+        bit *= 2
+    return blocks
+
+
+def doubled_up(x, axis, dim):
+    return joined_along(grow_blocks(x, axis), dim)
 
 
 def with_halo(shard, sides, width):
@@ -77,7 +98,7 @@
         rounded = direction.astype(jnp.bfloat16).reshape(local_bands, local_cells)
         partial_margin = lax.dot_general(
             occupied_rows,
-            lax.all_gather(rounded, "band", axis=0, tiled=True),
+            doubled_up(rounded, "band", 0),
             (((1,), (1,)), ((), ())),
             preferred_element_type=jnp.float32,
         )

time: 346 us -> 363 us (1.049)
  waiting for transfers between devices: 239 us -> 253 us
  starting transfers between devices: 9.07 us -> 16.6 us
  matrix products: 24 us -> 17.9 us
    ppermute x0 -> x4, waiting for transfers between devices: none -> 88.5 us  [grow_blocks(): other = lax.ppermute(blocks, axis, [(i, i ^ bit) for i in range(length)])]
    all_gather x2 -> x0, waiting for transfers between devices: 75.2 us -> none  [body(): lax.all_gather(rounded, 'band', axis=0, tiled=True)]
    ppermute x0 -> x4, starting transfers between devices: none -> 7.6 us  [grow_blocks(): other = lax.ppermute(blocks, axis, [(i, i ^ bit) for i in range(length)])]
    dot_general x2, matrix products: 11.7 us -> 5.66 us  [body(): lax.dot_general(occupied_rows, doubled_up(rounded, 'band', 0), (((1,), (1...]
  transfers between devices with their start and end apart: 10 -> 12, of which waited for: 8 -> 10; matrix products, arithmetic and copies ran while one was open for 0% -> 0% of each run, Pallas kernels for 0% -> 0%
where the time goes in v1:
time: 363 us; the launch traced here: 362 us
  waiting for transfers between devices  253 us (70%)
  blocking collectives  38.6 us (11%)
  other arithmetic  18.6 us (5%)
  matrix products  17.9 us (5%)
  starting transfers between devices  16.6 us (5%)
  between operations  14 us (4%)
  local copies, waits for them, and re-layouts  3.97 us (1%)
    psum x2, waiting for transfers between devices, body(): margins = lax.psum(partial_margin, 'grid')  104 us
    ppermute x4, waiting for transfers between devices, grow_blocks(): other = lax.ppermute(blocks, axis, [(i, i ^ bit) for i in range(length)])  88.5 us
    reduce_scatter x2, waiting for transfers between devices, body(): lax.psum_scatter(lax.dot_general(scaled, occupied_rows, (((0,), (0,)), ((...  57.9 us
    psum x1, blocking collectives, body(): curvature = lax.psum(inner_product(direction, applied), 'grid')  13.4 us
    psum x1, blocking collectives, body(): norm_now = lax.psum(inner_product(source_term, source_term), 'grid')  13.4 us
    dot_general x2, matrix products, body(): lax.dot_general(scaled, occupied_rows, (((0,), (0,)), ((), ())), preferre...  12.3 us
    psum x1, blocking collectives, body(): norm_next = lax.psum(inner_product(residual, residual), 'grid')  11.8 us
    ppermute x4, starting transfers between devices, grow_blocks(): other = lax.ppermute(blocks, axis, [(i, i ^ bit) for i in range(length)])  7.6 us
  transfers between devices with their start and end apart: 12, of which 10 were waited for; matrix products, arithmetic and copies ran while one was open for 0% of the time, Pallas kernels for 0%

profile of v1, /device:TPU:0, one launch (start us, length us, event | category | flops | bytes accessed | tf_op | source)
XLA Modules:
  0.0 362.4 jit_solution(9853384434465774333)
XLA Ops:
  8.6 3.1 collective-permute-start.2
  11.7 9.1 %collective-permute-done.2 = bf16[1,16,12288]{2,1,0:T(8,128)(2,1)S(1)} collective-permute-done((bf16[1,16,12288]{2,1,0:T(8,128)(2,1)S(1)}, bf16[1,16,12288]{2,1,0:T(8,128)(2,1)S(1)}, u32[]{:S(2)}, u32[]{:S(2)}) %collective-permute-start.2) | collective-permute-done | bytes 393248 | tf_op jit(solution)/shard_map/ppermute | solution.py:21
  20.9 2.8 collective-permute-start.3
  23.7 33.7 %collective-permute-done.3 = bf16[2,16,12288]{2,1,0:T(8,128)(2,1)S(1)} collective-permute-done((bf16[2,16,12288]{2,1,0:T(8,128)(2,1)S(1)}, bf16[2,16,12288]{2,1,0:T(8,128)(2,1)S(1)}, u32[]{:S(2)}, u32[]{:S(2)}) %collective-permute-start.3) | collective-permute-done | bytes 786464 | tf_op jit(solution)/shard_map/ppermute | solution.py:21
  57.7 2.5 copy-done
  60.3 2.8 fusion.10
  63.1 53.6 %all-reduce.6.cloned.1.call-done = f32[256,64]{0,1:T(8,128)} async-done(((f32[256,64]{0,1:T(8,128)}), f32[256,64]{0,1:T(8,128)}) %all-reduce.6.cloned.1.call-update) | async-done | bytes 65552 | tf_op jit(solution)/shard_map/psum | solution.py:105
  116.7 6.1 %convolution_convert_fusion.1 = bf16[64,12288]{1,0:T(8,128)(2,1)} fusion(bf16[32,8,96,128]{3,2,1,0:T(8,128)(2,1)} %bitcast.35, f32[256,64]{0,1:T(8,128)} %all-reduce.6.cloned.1.call-done), kind=kOutput, calls=%fused_computation.33 | convolution fusion | flops 403472384 | bytes 7929856 | tf_op jit(solution)/shard_map/dot_general | solution.py:108
  124.2 3.1 collective-permute-start
  128.8 28.9 %reduce-scatter.3.cloned.1.call-done = bf16[16,12288]{1,0:T(8,128)(2,1)} async-done(((bf16[64,12288]{1,0:T(8,128)(2,1)}), bf16[16,12288]{1,0:T(8,128)(2,1)}) %reduce-scatter.3.cloned.1.call-update) | async-done | bytes 393232 | tf_op jit(solution)/shard_map/reduce_scatter | solution.py:107
  158.9 3.0 multiply_reduce_fusion.2
  162.0 13.4 %all-reduce.2 = (f32[16]{0:T(128)S(1)}, f32[16]{0:T(128)S(1)}) all-reduce(f32[16]{0:T(128)S(1)} %get-tuple-element.3, f32[16]{0:T(128)S(1)} %get-tuple-element.2), channel_id=1, replica_groups=mesh['grid'=8,'band'=4] {'grid'}, use_global_device_ids=true, to_apply=%region_1.0 | all-reduce | flops 32 | bytes 256 | tf_op jit(solution)/shard_map/psum | solution.py:91
  176.8 11.8 %psum.45 = f32[16]{0:T(128)S(1)} all-reduce(f32[16]{0:T(128)S(1)} %multiply_reduce_fusion.1), channel_id=1, replica_groups=mesh['grid'=8,'band'=4] {'grid'}, use_global_device_ids=true, to_apply=%region_7.8 | all-reduce | flops 16 | bytes 128 | tf_op jit(solution)/shard_map/psum | solution.py:121
  188.6 2.4 fusion.89
  192.0 11.1 %collective-permute-done.6 = bf16[1,16,12288]{2,1,0:T(8,128)(2,1)S(1)} collective-permute-done((bf16[1,16,12288]{2,1,0:T(8,128)(2,1)}, bf16[1,16,12288]{2,1,0:T(8,128)(2,1)S(1)}, u32[]{:S(2)}, u32[]{:S(2)}) %collective-permute-start.6) | collective-permute-done | bytes 393248 | tf_op jit(solution)/shard_map/ppermute | solution.py:21
  205.9 34.6 %collective-permute-done.7 = bf16[2,16,12288]{2,1,0:T(8,128)(2,1)S(1)} collective-permute-done((bf16[2,16,12288]{2,1,0:T(8,128)(2,1)S(1)}, bf16[2,16,12288]{2,1,0:T(8,128)(2,1)S(1)}, u32[]{:S(2)}, u32[]{:S(2)}) %collective-permute-start.7) | collective-permute-done | bytes 786464 | tf_op jit(solution)/shard_map/ppermute | solution.py:21
  240.8 2.9 fusion.13
  243.9 50.0 %all-reduce.8.cloned.1.call-done = f32[256,64]{0,1:T(8,128)} async-done(((f32[256,64]{0,1:T(8,128)}), f32[256,64]{0,1:T(8,128)}) %all-reduce.8.cloned.1.call-update) | async-done | bytes 65552 | tf_op jit(solution)/shard_map/psum | solution.py:105
  293.9 6.1 %convolution_convert_fusion = bf16[64,12288]{1,0:T(8,128)(2,1)} fusion(bf16[32,8,96,128]{3,2,1,0:T(8,128)(2,1)} %bitcast.36, f32[256,64]{0,1:T(8,128)} %all-reduce.8.cloned.1.call-done), kind=kOutput, calls=%fused_computation.32 | convolution fusion | flops 403472384 | bytes 7929856 | tf_op jit(solution)/shard_map/dot_general | solution.py:108
  301.3 3.1 collective-permute-start.4
  305.9 29.0 %reduce-scatter.5.cloned.1.call-done = bf16[16,12288]{1,0:T(8,128)(2,1)} async-done(((bf16[64,12288]{1,0:T(8,128)(2,1)}), bf16[16,12288]{1,0:T(8,128)(2,1)}) %reduce-scatter.5.cloned.1.call-update) | async-done | bytes 393232 | tf_op jit(solution)/shard_map/reduce_scatter | solution.py:107
  336.2 3.1 multiply_reduce_fusion
  339.3 13.4 %psum.47 = f32[16]{0:T(128)S(1)} all-reduce(f32[16]{0:T(128)S(1)} %get-tuple-element.6), channel_id=1, replica_groups=mesh['grid'=8,'band'=4] {'grid'}, use_global_device_ids=true, to_apply=%region_11.12 | all-reduce | flops 16 | bytes 128 | tf_op jit(solution)/shard_map/psum | solution.py:116
  352.7 3.2 multiply_subtract_fusion
  (53 shorter events, 15.6 us)
Async XLA Ops:
  7.2 109.5 %all-reduce.6.cloned.1.call-start = ((), (), s32[]{:S(2)}) async-start(), calls=%async_computation.2 | async-start | bytes 131072 | tf_op jit(solution)/shard_map/psum | solution.py:105
  8.6 12.2 %collective-permute-start.2 = (bf16[1,16,12288]{2,1,0:T(8,128)(2,1)S(1)}, bf16[1,16,12288]{2,1,0:T(8,128)(2,1)S(1)}, u32[]{:S(2)}, u32[]{:S(2)}) collective-permute-start(bf16[1,16,12288]{2,1,0:T(8,128)(2,1)S(1)} %broadcast_in_dim_reshape.6), channel_id=1, source_target_pairs={{0,1},{1,0},{2,3},{3,2},{4,5},{5,4},{6,7},{7,6},{8,9},{9,8},{10,11... | collective-permute-start | bytes 1179656 | tf_op jit(solution)/shard_map/ppermute | solution.py:21
  20.9 36.5 %collective-permute-start.3 = (bf16[2,16,12288]{2,1,0:T(8,128)(2,1)S(1)}, bf16[2,16,12288]{2,1,0:T(8,128)(2,1)S(1)}, u32[]{:S(2)}, u32[]{:S(2)}) collective-permute-start(bf16[2,16,12288]{2,1,0:T(8,128)(2,1)S(1)} %pad_maximum_fusion.2), channel_id=1, source_target_pairs={{0,2},{1,3},{2,0},{3,1},{4,6},{5,7},{6,4},{7,5},{8,10},{9,11},{10,... | collective-permute-start | bytes 2359304 | tf_op jit(solution)/shard_map/ppermute | solution.py:21
  57.5 2.8 copy-start
  63.1 94.6 %reduce-scatter.3.cloned.1.call-start = ((), (), s32[]{:S(2)}) async-start(), calls=%async_computation.3 | async-start | bytes 1966080 | tf_op jit(solution)/shard_map/reduce_scatter | solution.py:107
  122.8 171.0 %all-reduce.8.cloned.1.call-start = ((), (), s32[]{:S(2)}) async-start(), calls=%async_computation.4 | async-start | bytes 131072 | tf_op jit(solution)/shard_map/psum | solution.py:105
  122.9 4.4 %collective-permute-start.1 = (bf16[16,4,24,128]{3,2,1,0:T(8,128)(2,1)S(1)}, bf16[16,4,24,128]{3,2,1,0:T(8,128)(2,1)S(1)}, u32[]{:S(2)}, u32[]{:S(2)}) collective-permute-start(bf16[16,4,24,128]{3,2,1,0:T(8,128)(2,1)S(1)} %convert_element_type.31), channel_id=1, source_target_pairs={{4,0},{8,4},{12,8},{16,12},{20,16},{24,20},{28,24},{5,1},{9,5},{13... | collective-permute-start | bytes 1179656 | tf_op jit(solution)/shard_map/ppermute | solution.py:40
  124.2 4.4 %collective-permute-start = (bf16[16,4,24,128]{3,2,1,0:T(8,128)(2,1)S(1)}, bf16[16,4,24,128]{3,2,1,0:T(8,128)(2,1)S(1)}, u32[]{:S(2)}, u32[]{:S(2)}) collective-permute-start(bf16[16,4,24,128]{3,2,1,0:T(8,128)(2,1)S(1)} %convert_element_type.31), channel_id=1, source_target_pairs={{0,4},{4,8},{8,12},{12,16},{16,20},{20,24},{24,28},{1,5},{5,9},{9,... | collective-permute-start | bytes 1179656 | tf_op jit(solution)/shard_map/ppermute | solution.py:39
  128.7 30.2 %copy-start.1 = (f32[16,4,24,128]{3,2,1,0:T(8,128)S(1)}, f32[16,4,24,128]{3,2,1,0:T(8,128)}, u32[]{:S(2)}) copy-start(f32[16,4,24,128]{3,2,1,0:T(8,128)} %param.7) | copy-start | bytes 2359300
  128.7 30.2 %copy-start.3 = (f32[4,24,128]{2,1,0:T(8,128)S(1)}, f32[4,24,128]{2,1,0:T(8,128)}, u32[]{:S(2)}) copy-start(f32[4,24,128]{2,1,0:T(8,128)} %param.5) | copy-start | bytes 147460
  128.8 30.2 %copy-start.5 = (f32[16]{0:T(128)S(1)}, f32[16]{0:T(128)}, u32[]{:S(2)}) copy-start(f32[16]{0:T(128)} %param.6) | copy-start | bytes 196
  188.6 52.1 %slice-start = ((s8[6291456]{0:T(1024)(128)(4,1)}), s8[2097152]{0:T(1024)(128)(4,1)S(1)}, s32[]{:S(2)}) async-start(s8[6291456]{0:T(1024)(128)(4,1)} %bitcast.38), calls=%async_computation.6 | async-start | bytes 4194304
  192.0 11.1 %collective-permute-start.6 = (bf16[1,16,12288]{2,1,0:T(8,128)(2,1)}, bf16[1,16,12288]{2,1,0:T(8,128)(2,1)S(1)}, u32[]{:S(2)}, u32[]{:S(2)}) collective-permute-start(bf16[1,16,12288]{2,1,0:T(8,128)(2,1)} %broadcast_in_dim_reshape.7), channel_id=1, source_target_pairs={{0,1},{1,0},{2,3},{3,2},{4,5},{5,4},{6,7},{7,6},{8,9},{9,8},{10,11... | collective-permute-start | bytes 1179656 | tf_op jit(solution)/shard_map/ppermute | solution.py:21
  204.1 36.6 %slice-start.1 = ((s8[6291456]{0:T(1024)(128)(4,1)}), s8[4194304]{0:T(1024)(128)(4,1)S(1)}, s32[]{:S(2)}) async-start(s8[6291456]{0:T(1024)(128)(4,1)} %bitcast.38), calls=%async_computation.7 | async-start | bytes 8388608
  204.2 36.3 %collective-permute-start.7 = (bf16[2,16,12288]{2,1,0:T(8,128)(2,1)S(1)}, bf16[2,16,12288]{2,1,0:T(8,128)(2,1)S(1)}, u32[]{:S(2)}, u32[]{:S(2)}) collective-permute-start(bf16[2,16,12288]{2,1,0:T(8,128)(2,1)S(1)} %pad_maximum_fusion.3), channel_id=1, source_target_pairs={{0,2},{1,3},{2,0},{3,1},{4,6},{5,7},{6,4},{7,5},{8,10},{9,11},{10,... | collective-permute-start | bytes 2359304 | tf_op jit(solution)/shard_map/ppermute | solution.py:21
  243.7 91.2 %reduce-scatter.5.cloned.1.call-start = ((), (), s32[]{:S(2)}) async-start(), calls=%async_computation.5 | async-start | bytes 1966080 | tf_op jit(solution)/shard_map/reduce_scatter | solution.py:107
  300.0 4.4 %collective-permute-start.5 = (bf16[16,4,24,128]{3,2,1,0:T(8,128)(2,1)S(1)}, bf16[16,4,24,128]{3,2,1,0:T(8,128)(2,1)S(1)}, u32[]{:S(2)}, u32[]{:S(2)}) collective-permute-start(bf16[16,4,24,128]{3,2,1,0:T(8,128)(2,1)S(1)} %get-tuple-element.8), channel_id=1, source_target_pairs={{4,0},{8,4},{12,8},{16,12},{20,16},{24,20},{28,24},{5,1},{9,5},{13... | collective-permute-start | bytes 1179656 | tf_op jit(solution)/shard_map/ppermute | solution.py:40
  301.3 4.4 %collective-permute-start.4 = (bf16[16,4,24,128]{3,2,1,0:T(8,128)(2,1)S(1)}, bf16[16,4,24,128]{3,2,1,0:T(8,128)(2,1)S(1)}, u32[]{:S(2)}, u32[]{:S(2)}) collective-permute-start(bf16[16,4,24,128]{3,2,1,0:T(8,128)(2,1)S(1)} %get-tuple-element.8), channel_id=1, source_target_pairs={{0,4},{4,8},{8,12},{12,16},{16,20},{20,24},{24,28},{1,5},{5,9},{9,... | collective-permute-start | bytes 1179656 | tf_op jit(solution)/shard_map/ppermute | solution.py:39
  305.9 30.3 %copy-start.4 = (f32[4,24,128]{2,1,0:T(8,128)S(1)}, f32[4,24,128]{2,1,0:T(8,128)}, u32[]{:S(2)}) copy-start(f32[4,24,128]{2,1,0:T(8,128)} %param.5) | copy-start | bytes 147460
  334.9 1.3 copy-start.2
Sparse Core Ops, SparseCore 0:
  63.2 53.4 all-reduce.5
  123.0 34.6 reduce-scatter.2
  243.8 50.0 all-reduce.7
  300.1 34.6 reduce-scatter.4
